TPU v7x, 512 devices: a whole 4x8x8 slice. The times are simulated.
512 devices in a mesh: wide: 32 (over z, x), narrow: 16 (over y, core).
Axes of the slice: x: 4, y: 8, z: 8, core: 2. Of those that a mesh axis runs over, the one named last changes fastest.
Arguments:
- tokens: bfloat16 [1024, 16384], P('wide', 'narrow'), may hold values from -200 to 200
- norm_gain: float32 [16384], P('narrow'), may hold values from 0.25 to 1.75
- gate_weight: bfloat16 [26624, 16384], P('wide', 'narrow'), may hold values from -0.046875 to 0.046875
- up_weight: bfloat16 [26624, 16384], P('wide', 'narrow'), may hold values from -0.046875 to 0.046875
- down_weight: bfloat16 [26624, 16384], P('wide', 'narrow'), may hold values from -0.0390625 to 0.0390625
Outputs:
- ffn_out: bfloat16 [1024, 16384], P('wide', 'narrow')
All inputs are finite; a program needn't handle non-finite values.
Results may differ from a plain program's by a relative error of at most 0.03.
Values may be sent and summed in bfloat16 or wider, within the bound.
No kernel may reach another device: no remote copies, remote signals or barrier semaphores. Data moves between devices by JAX's collectives and lax.ppermute only.
A program may use at most 64 MiB of HBM per device.

v0:
```python
import jax
import jax.numpy as jnp
from jax import lax
from jax.sharding import Mesh, PartitionSpec as P

EPS = 1e-05
NARROW = ("y", "core")


def local(tokens, norm_gain, gate_weight, up_weight, down_weight):
    width = gate_weight.shape[0]
    n_z = lax.axis_size("z")
    n_x = lax.axis_size("x")
    n_narrow = lax.axis_size(NARROW)
    model_width = tokens.shape[1] * n_narrow
    rows = tokens.shape[0]
    spread = jnp.broadcast_to(tokens[None], (n_z,) + tokens.shape)
    near = lax.all_to_all(spread, "z", 0, 0)
    spread = jnp.broadcast_to(near[:, None], (n_z, n_x) + tokens.shape)
    whole = lax.all_to_all(spread, "x", 1, 1).reshape(n_z * n_x * rows, tokens.shape[1])
    values = whole.astype(jnp.float32)
    partial = jnp.sum(values * values, axis=1)
    scaled = (values * norm_gain).astype(jnp.bfloat16)
    dims = (((1,), (1,)), ((), ()))
    joined = jnp.concatenate([gate_weight, up_weight], axis=0)
    pair = lax.dot_general(scaled, joined, dims, preferred_element_type=jnp.float32).astype(
        jnp.bfloat16
    )
    n_y = lax.axis_size("y")
    n_c = lax.axis_size("core")
    step = pair.shape[0] // (n_y * n_c)
    pieces = pair.reshape(n_y, n_c, step, pair.shape[1])
    inner = jnp.sum(lax.all_to_all(pieces, "core", 1, 1).astype(jnp.float32), axis=1).astype(
        jnp.bfloat16
    )
    part = jnp.sum(lax.all_to_all(inner, "y", 0, 0).astype(jnp.float32), axis=0)
    shares = partial.reshape(n_y, n_c, step)
    shares = jnp.sum(lax.all_to_all(shares, "core", 1, 1), axis=1)
    mine_sq = jnp.sum(lax.all_to_all(shares, "y", 0, 0), axis=0)
    scale = lax.rsqrt(mine_sq / model_width + EPS)[:, None]
    sums = part.astype(jnp.float32)
    mine = (jax.nn.silu(sums[:, :width] * scale) * (sums[:, width:] * scale)).astype(jnp.bfloat16)
    half = width // 2
    first = lax.all_gather(mine[:, :half], NARROW, axis=0, tiled=True)
    second = lax.all_gather(mine[:, half:], NARROW, axis=0, tiled=True)
    down = (
        jnp.dot(first, down_weight[:half], preferred_element_type=jnp.float32)
        + jnp.dot(second, down_weight[half:], preferred_element_type=jnp.float32)
    ).astype(jnp.bfloat16)
    pieces = down.reshape(n_z, n_x, rows, down.shape[1])
    across = jnp.sum(lax.all_to_all(pieces, "x", 1, 1).astype(jnp.float32), axis=1).astype(
        jnp.bfloat16
    )
    return jnp.sum(lax.all_to_all(across, "z", 0, 0).astype(jnp.float32), axis=0).astype(
        jnp.bfloat16
    )


def solution(mesh):
    n_wide, n_narrow = mesh.devices.shape
    n_x = len({device.coords[0] for device in mesh.devices[:, 0]})
    view = Mesh(mesh.devices.reshape(n_wide // n_x, n_x, n_narrow // 2, 2), ("z", "x", "y", "core"))
    wide = ("z", "x")
    in_specs = (P(wide, NARROW), P(NARROW), P(wide, NARROW), P(wide, NARROW), P(wide, NARROW))
    out_specs = P(wide, NARROW)
    return jax.shard_map(local, mesh=view, in_specs=in_specs, out_specs=out_specs, check_vma=False)
```

profile of v0, /device:TPU:2, one launch (start us, length us, event | category | flops | bytes accessed | tf_op | source)
XLA Modules:
  0.0 226.4 jit_solution(4716993163845403259)
XLA Ops:
  0.0 0.9 broadcast_in_dim.4
  0.9 27.6 %all_to_all.44 = bf16[8,32,1024]{2,1,0:T(8,128)(2,1)S(1)} all-to-all(bf16[8,32,1024]{2,1,0:T(8,128)(2,1)S(1)} %broadcast_in_dim.4), channel_id=1, replica_groups=mesh['z'=8,'x'=4,'y'=8,'core'=2] {'z'}, dimensions={0} | all-to-all | bytes 1048576 | tf_op jit(solution)/shard_map/all_to_all | solution.py:18
  28.5 0.3 broadcast_in_dim.5
  28.8 27.7 %all_to_all.45 = bf16[8,4,32,1024]{3,2,0,1:T(8,128)(2,1)S(1)} all-to-all(bf16[8,4,32,1024]{3,2,0,1:T(8,128)(2,1)S(1)} %broadcast_in_dim.5), channel_id=1, replica_groups=mesh['z'=8,'x'=4,'y'=8,'core'=2] {'x'}, dimensions={1} | all-to-all | bytes 4194304 | tf_op jit(solution)/shard_map/all_to_all | solution.py:20
  56.5 0.5 multiply_reduce_fusion
  57.0 0.1 reshape.25
  57.1 0.1 reshape.28
  57.1 3.7 %all_to_all.46 = f32[2,1,512]{2,1,0:T(1,128)S(1)} all-to-all(f32[2,1,512]{2,1,0:T(1,128)S(1)} %reshape.28), channel_id=1, replica_groups=mesh['z'=8,'x'=4,'y'=8,'core'=2] {'core'}, dimensions={0} | all-to-all | bytes 8192 | tf_op jit(solution)/shard_map/all_to_all | solution.py:38
  60.8 0.5 broadcast.14
  61.3 0.7 reduce.5
  62.0 0.1 reshape.29
  62.1 0.6 bitcast_reduce_fusion
  62.7 0.0 copy-start.1
  62.7 0.5 copy_convert_fusion
  63.2 0.2 copy-done.1
  63.4 0.0 copy-start.2
  63.4 0.0 copy-start.3
  63.4 0.6 fusion
  64.0 0.8 copy-done.2
  64.8 0.5 copy-done.3
  65.3 4.2 %convolution_convert_fusion = bf16[1024,1664]{1,0:T(8,128)(2,1)S(1)} fusion(bf16[1024,1024]{1,0:T(8,128)(2,1)S(1)} %fusion, bf16[832,1024]{1,0:T(8,128)(2,1)S(1)} %copy-done.2, bf16[832,1024]{1,0:T(8,128)(2,1)S(1)} %copy-done.3), kind=kOutput, calls=%fused_computation.4 | convolution fusion | flops 3498180608 | bytes 8912896 | tf_op jit(solution)/shard_map/dot_general | solution.py:26
  69.6 0.3 copy.13
  69.8 6.5 %all_to_all.47 = bf16[8,2,64,1664]{3,2,0,1:T(8,128)(2,1)S(1)} all-to-all(bf16[8,2,64,1664]{3,2,0,1:T(8,128)(2,1)S(1)} %copy.13), channel_id=1, replica_groups=mesh['z'=8,'x'=4,'y'=8,'core'=2] {'core'}, dimensions={1} | all-to-all | bytes 6815744 | tf_op jit(solution)/shard_map/all_to_all | solution.py:33
  76.3 7.1 %all-to-all-start.5 = ((f32[8,1,64]{2,1,0:T(1,128)}), f32[8,1,64]{2,1,0:T(1,128)S(1)}, u32[]{:S(2)}, u32[]{:S(2)}) async-start(f32[8,1,64]{2,1,0:T(1,128)} %bitcast.2), calls=%async_computation.5 | async-start | bytes 8192 | tf_op jit(solution)/shard_map/all_to_all | solution.py:39
  83.4 2.3 %reduce_sum.72 = bf16[8,64,1664]{2,1,0:T(8,128)(2,1)} reduce(bf16[8,2,64,1664]{3,2,0,1:T(8,128)(2,1)S(1)} %all_to_all.47, bf16[]{:T(256)} %constant.9.clone.1), dimensions={1}, to_apply=%region_0.0 | reduce | flops 851968 | bytes 5111810 | tf_op jit(solution)/shard_map/reduce_sum | solution.py:33
  85.7 5.3 %all-to-all-done.5 = f32[8,1,64]{2,1,0:T(1,128)S(1)} async-done(((f32[8,1,64]{2,1,0:T(1,128)}), f32[8,1,64]{2,1,0:T(1,128)S(1)}, u32[]{:S(2)}, u32[]{:S(2)}) %all-to-all-start.5) | async-done | bytes 2080 | tf_op jit(solution)/shard_map/all_to_all | solution.py:39
  91.0 3.6 %all-to-all-start.3 = ((bf16[8,64,1664]{2,1,0:T(8,128)(2,1)}), bf16[8,64,1664]{2,1,0:T(8,128)(2,1)S(1)}, u32[]{:S(2)}, u32[]{:S(2)}) async-start(bf16[8,64,1664]{2,1,0:T(8,128)(2,1)} %reduce_sum.72), calls=%async_computation.3 | async-start | bytes 3407872 | tf_op jit(solution)/shard_map/all_to_all | solution.py:36
  94.7 0.0 copy-start
  94.7 41.8 %all-to-all-done.3 = bf16[8,64,1664]{2,1,0:T(8,128)(2,1)S(1)} async-done(((bf16[8,64,1664]{2,1,0:T(8,128)(2,1)}), bf16[8,64,1664]{2,1,0:T(8,128)(2,1)S(1)}, u32[]{:S(2)}, u32[]{:S(2)}) %all-to-all-start.3) | async-done | bytes 1703968 | tf_op jit(solution)/shard_map/all_to_all | solution.py:36
  136.5 0.2 convert_reduce_fusion
  136.7 0.1 fusion.8
  136.9 0.1 fusion.10
  137.0 17.6 %all_gather.7 = bf16[1024,416]{1,0:T(8,128)(2,1)S(1)} all-gather(bf16[64,416]{1,0:T(8,128)(2,1)S(1)} %get-tuple-element.5), channel_id=1, replica_groups=mesh['z'=8,'x'=4,'y'=8,'core'=2] {'y','core'}, dimensions={0}, use_global_device_ids=true | all-gather | bytes 905216 | tf_op jit(solution)/shard_map/all_gather | solution.py:45
  154.6 18.6 %all_gather.6 = bf16[1024,416]{1,0:T(8,128)(2,1)S(1)} all-gather(bf16[64,416]{1,0:T(8,128)(2,1)S(1)} %get-tuple-element.6), channel_id=1, replica_groups=mesh['z'=8,'x'=4,'y'=8,'core'=2] {'y','core'}, dimensions={0}, use_global_device_ids=true | all-gather | bytes 905216 | tf_op jit(solution)/shard_map/all_gather | solution.py:44
  173.2 0.0 copy-done
  173.2 1.3 fusion.5
  174.5 1.3 add_convert_fusion
  175.8 0.3 copy.15
  176.1 29.6 %all_to_all.48 = bf16[8,4,32,1024]{3,2,0,1:T(8,128)(2,1)S(1)} all-to-all(bf16[8,4,32,1024]{3,2,0,1:T(8,128)(2,1)S(1)} %copy.15), channel_id=1, replica_groups=mesh['z'=8,'x'=4,'y'=8,'core'=2] {'x'}, dimensions={1} | all-to-all | bytes 4194304 | tf_op jit(solution)/shard_map/all_to_all | solution.py:51
  205.7 0.4 reduce_sum.77
  206.1 19.7 %all_to_all.49 = bf16[8,32,1024]{2,1,0:T(8,128)(2,1)S(1)} all-to-all(bf16[8,32,1024]{2,1,0:T(8,128)(2,1)S(1)} %reduce_sum.77), channel_id=1, replica_groups=mesh['z'=8,'x'=4,'y'=8,'core'=2] {'z'}, dimensions={0} | all-to-all | bytes 1048576 | tf_op jit(solution)/shard_map/all_to_all | solution.py:54
  225.7 0.7 reduce_sum.78
  (3 shorter events, 0.0 us)
Async XLA Ops:
  62.7 0.7 copy-start.1
  63.4 1.5 copy-start.2
  63.4 2.0 copy-start.3
  76.3 14.7 %all-to-all-start.5 = ((f32[8,1,64]{2,1,0:T(1,128)}), f32[8,1,64]{2,1,0:T(1,128)S(1)}, u32[]{:S(2)}, u32[]{:S(2)}) async-start(f32[8,1,64]{2,1,0:T(1,128)} %bitcast.2), calls=%async_computation.5 | async-start | bytes 8192 | tf_op jit(solution)/shard_map/all_to_all | solution.py:39
  91.0 45.5 %all-to-all-start.3 = ((bf16[8,64,1664]{2,1,0:T(8,128)(2,1)}), bf16[8,64,1664]{2,1,0:T(8,128)(2,1)S(1)}, u32[]{:S(2)}, u32[]{:S(2)}) async-start(bf16[8,64,1664]{2,1,0:T(8,128)(2,1)} %reduce_sum.72), calls=%async_computation.3 | async-start | bytes 3407872 | tf_op jit(solution)/shard_map/all_to_all | solution.py:36
  94.7 78.6 %copy-start = (bf16[832,1024]{1,0:T(8,128)(2,1)S(1)}, bf16[832,1024]{1,0:T(8,128)(2,1)}, u32[]{:S(2)}) copy-start(bf16[832,1024]{1,0:T(8,128)(2,1)} %param.9) | copy-start | bytes 5111812
where the time goes:
time: 227 us; the launch traced here: 226 us
  blocking collectives  151 us (67%)
  waiting for transfers between devices  47.2 us (21%)
  starting transfers between devices  10.7 us (5%)
  matrix products  6.75 us (3%)
  other arithmetic  6.62 us (3%)
  local copies, waits for them, and re-layouts  4.1 us (2%)
    all_to_all x1, waiting for transfers between devices, local(): part = jnp.sum(lax.all_to_all(inner, 'y', 0, 0).astype(jnp.float32), axis=0)  41.8 us
    all_to_all x1, blocking collectives, local(): lax.all_to_all(pieces, 'x', 1, 1).astype(jnp.float32)  29.6 us
    all_to_all x1, blocking collectives, local(): lax.all_to_all(spread, 'x', 1, 1).reshape(n_z * n_x * rows, tokens.shape[1])  27.7 us
    all_to_all x1, blocking collectives, local(): near = lax.all_to_all(spread, 'z', 0, 0)  27.6 us
    all_to_all x1, blocking collectives, local(): lax.all_to_all(across, 'z', 0, 0).astype(jnp.float32)  19.7 us
    all_gather x1, blocking collectives, local(): first = lax.all_gather(mine[:, :half], NARROW, axis=0, tiled=True)  18.6 us
    all_gather x1, blocking collectives, local(): second = lax.all_gather(mine[:, half:], NARROW, axis=0, tiled=True)  17.6 us
    all_to_all x1, starting transfers between devices, local(): mine_sq = jnp.sum(lax.all_to_all(shares, 'y', 0, 0), axis=0)  7.1 us
  transfers between devices with their start and end apart: 2, of which 2 were waited for; matrix products, arithmetic and copies ran while one was open for 1% of the time, Pallas kernels for 0%

commit v1 on v0

--- a/solution.py
+++ b/solution.py
@@ -42,7 +42,9 @@
     mine = (jax.nn.silu(sums[:, :width] * scale) * (sums[:, width:] * scale)).astype(jnp.bfloat16)
     half = width // 2
     first = lax.all_gather(mine[:, :half], NARROW, axis=0, tiled=True)
-    second = lax.all_gather(mine[:, half:], NARROW, axis=0, tiled=True)
+    second = jnp.concatenate(
+        lax.all_to_all(jnp.stack([mine[:, half:]] * lax.axis_size(NARROW)), NARROW, 0, 0), axis=0
+    )
     down = (
         jnp.dot(first, down_weight[:half], preferred_element_type=jnp.float32)
         + jnp.dot(second, down_weight[half:], preferred_element_type=jnp.float32)

time: 227 us -> 240 us (1.057)
  matrix products: 6.75 us -> 10.9 us
  blocking collectives: 151 us -> 155 us
  starting transfers between devices: 10.7 us -> 14.3 us
    all_gather x1, blocking collectives: 18.6 us -> 40.5 us  [local(): first = lax.all_gather(mine[:, :half], NARROW, axis=0, tiled=True)]
    all_gather x1 -> x0, blocking collectives: 17.6 us -> none  [local(): second = lax.all_gather(mine[:, half:], NARROW, axis=0, tiled=True)]
    all_to_all x0 -> x1, starting transfers between devices: none -> 3.65 us  [local(): lax.all_to_all(jnp.stack([mine[:, half:]] * lax.axis_size(NARROW)), NARRO...]
  transfers between devices with their start and end apart: 2 -> 3, of which waited for: 2 -> 2; matrix products, arithmetic and copies ran while one was open for 1% -> 2% of each run, Pallas kernels for 0% -> 0%
where the time goes in v1:
time: 240 us
  blocking collectives  155 us (65%)
  waiting for transfers between devices  47.2 us (20%)
  starting transfers between devices  14.3 us (6%)
  matrix products  10.9 us (5%)
  other arithmetic  6.62 us (3%)
  local copies, waits for them, and re-layouts  5.18 us (2%)
    all_to_all x1, waiting for transfers between devices, local(): part = jnp.sum(lax.all_to_all(inner, 'y', 0, 0).astype(jnp.float32), axis=0)  41.8 us
    all_gather x1, blocking collectives, local(): first = lax.all_gather(mine[:, :half], NARROW, axis=0, tiled=True)  40.5 us
    all_to_all x1, blocking collectives, local(): lax.all_to_all(pieces, 'x', 1, 1).astype(jnp.float32)  29.6 us
    all_to_all x1, blocking collectives, local(): lax.all_to_all(spread, 'x', 1, 1).reshape(n_z * n_x * rows, tokens.shape[1])  27.7 us
    all_to_all x1, blocking collectives, local(): near = lax.all_to_all(spread, 'z', 0, 0)  27.6 us
    all_to_all x1, blocking collectives, local(): lax.all_to_all(across, 'z', 0, 0).astype(jnp.float32)  19.7 us
    all_to_all x1, starting transfers between devices, local(): mine_sq = jnp.sum(lax.all_to_all(shares, 'y', 0, 0), axis=0)  7.1 us
    all_to_all x1, blocking collectives, local(): lax.all_to_all(pieces, 'core', 1, 1).astype(jnp.float32)  6.47 us
  transfers between devices with their start and end apart: 3, of which 2 were waited for; matrix products, arithmetic and copies ran while one was open for 2% of the time, Pallas kernels for 0%

profile of v1, /device:TPU:2, one launch (start us, length us, event | category | flops | bytes accessed | tf_op | source)
XLA Modules:
  0.0 239.5 jit_solution(8470520324391888589)
XLA Ops:
  0.0 0.9 broadcast_in_dim.4
  0.9 27.6 %all_to_all.49 = bf16[8,32,1024]{2,1,0:T(8,128)(2,1)S(1)} all-to-all(bf16[8,32,1024]{2,1,0:T(8,128)(2,1)S(1)} %broadcast_in_dim.4), channel_id=1, replica_groups=mesh['z'=8,'x'=4,'y'=8,'core'=2] {'z'}, dimensions={0} | all-to-all | bytes 1048576 | tf_op jit(solution)/shard_map/all_to_all | solution.py:18
  28.5 0.3 broadcast_in_dim.5
  28.8 27.7 %all_to_all.50 = bf16[8,4,32,1024]{3,2,0,1:T(8,128)(2,1)S(1)} all-to-all(bf16[8,4,32,1024]{3,2,0,1:T(8,128)(2,1)S(1)} %broadcast_in_dim.5), channel_id=1, replica_groups=mesh['z'=8,'x'=4,'y'=8,'core'=2] {'x'}, dimensions={1} | all-to-all | bytes 4194304 | tf_op jit(solution)/shard_map/all_to_all | solution.py:20
  56.5 0.5 multiply_reduce_fusion
  57.0 0.1 reshape.30
  57.1 0.1 reshape.34
  57.1 3.7 %all_to_all.51 = f32[2,1,512]{2,1,0:T(1,128)S(1)} all-to-all(f32[2,1,512]{2,1,0:T(1,128)S(1)} %reshape.34), channel_id=1, replica_groups=mesh['z'=8,'x'=4,'y'=8,'core'=2] {'core'}, dimensions={0} | all-to-all | bytes 8192 | tf_op jit(solution)/shard_map/all_to_all | solution.py:38
  60.8 0.5 broadcast.16
  61.3 0.7 reduce.5
  62.0 0.1 reshape.35
  62.1 0.6 bitcast_reduce_fusion
  62.7 0.0 copy-start.1
  62.7 0.5 copy_convert_fusion
  63.2 0.2 copy-done.1
  63.4 0.0 copy-start.2
  63.4 0.0 copy-start.3
  63.4 0.6 fusion
  64.0 0.8 copy-done.2
  64.8 0.5 copy-done.3
  65.3 4.2 %convolution_convert_fusion = bf16[1024,1664]{1,0:T(8,128)(2,1)S(1)} fusion(bf16[1024,1024]{1,0:T(8,128)(2,1)S(1)} %fusion, bf16[832,1024]{1,0:T(8,128)(2,1)S(1)} %copy-done.2, bf16[832,1024]{1,0:T(8,128)(2,1)S(1)} %copy-done.3), kind=kOutput, calls=%fused_computation.4 | convolution fusion | flops 3498180608 | bytes 8912896 | tf_op jit(solution)/shard_map/dot_general | solution.py:26
  69.6 0.3 copy.13
  69.8 6.5 %all_to_all.52 = bf16[8,2,64,1664]{3,2,0,1:T(8,128)(2,1)S(1)} all-to-all(bf16[8,2,64,1664]{3,2,0,1:T(8,128)(2,1)S(1)} %copy.13), channel_id=1, replica_groups=mesh['z'=8,'x'=4,'y'=8,'core'=2] {'core'}, dimensions={1} | all-to-all | bytes 6815744 | tf_op jit(solution)/shard_map/all_to_all | solution.py:33
  76.3 7.1 %all-to-all-start.5 = ((f32[8,1,64]{2,1,0:T(1,128)}), f32[8,1,64]{2,1,0:T(1,128)S(1)}, u32[]{:S(2)}, u32[]{:S(2)}) async-start(f32[8,1,64]{2,1,0:T(1,128)} %bitcast.2), calls=%async_computation.5 | async-start | bytes 8192 | tf_op jit(solution)/shard_map/all_to_all | solution.py:39
  83.4 2.3 reduce_sum.72
  85.7 5.3 %all-to-all-done.5 = f32[8,1,64]{2,1,0:T(1,128)S(1)} async-done(((f32[8,1,64]{2,1,0:T(1,128)}), f32[8,1,64]{2,1,0:T(1,128)S(1)}, u32[]{:S(2)}, u32[]{:S(2)}) %all-to-all-start.5) | async-done | bytes 2080 | tf_op jit(solution)/shard_map/all_to_all | solution.py:39
  91.0 3.6 %all-to-all-start.3 = ((bf16[8,64,1664]{2,1,0:T(8,128)(2,1)}), bf16[8,64,1664]{2,1,0:T(8,128)(2,1)S(1)}, u32[]{:S(2)}, u32[]{:S(2)}) async-start(bf16[8,64,1664]{2,1,0:T(8,128)(2,1)} %reduce_sum.72), calls=%async_computation.3 | async-start | bytes 3407872 | tf_op jit(solution)/shard_map/all_to_all | solution.py:36
  94.7 41.8 %all-to-all-done.3 = bf16[8,64,1664]{2,1,0:T(8,128)(2,1)S(1)} async-done(((bf16[8,64,1664]{2,1,0:T(8,128)(2,1)}), bf16[8,64,1664]{2,1,0:T(8,128)(2,1)S(1)}, u32[]{:S(2)}, u32[]{:S(2)}) %all-to-all-start.3) | async-done | bytes 1703968 | tf_op jit(solution)/shard_map/all_to_all | solution.py:36
  136.5 0.2 convert_reduce_fusion
  136.7 0.1 fusion.8
  136.9 0.1 fusion.10
  137.0 0.0 copy-start
  137.0 1.1 stack.2
  138.1 3.7 %all-to-all-start.6 = ((bf16[16,64,416]{2,1,0:T(8,128)(2,1)}), bf16[16,64,416]{2,1,0:T(8,128)(2,1)S(1)}, u32[]{:S(2)}, u32[]{:S(2)}) async-start(bf16[16,64,416]{2,1,0:T(8,128)(2,1)} %stack.2), calls=%async_computation.6 | async-start | bytes 2097152 | tf_op jit(solution)/shard_map/all_to_all | solution.py:46
  141.7 40.5 %all_gather.3 = bf16[1024,416]{1,0:T(8,128)(2,1)S(1)} all-gather(bf16[64,416]{1,0:T(8,128)(2,1)S(1)} %get-tuple-element.6), channel_id=1, replica_groups=mesh['z'=8,'x'=4,'y'=8,'core'=2] {'y','core'}, dimensions={0}, use_global_device_ids=true | all-gather | bytes 905216 | tf_op jit(solution)/shard_map/all_gather | solution.py:44
  182.2 0.0 copy-done
  182.2 3.2 %fusion.5 = f32[1024,1024]{1,0:T(8,128)} fusion(bf16[1024,416]{1,0:T(8,128)(2,1)S(1)} %all_gather.3, bf16[832,1024]{1,0:T(8,128)(2,1)S(1)} %copy-done), kind=kOutput, calls=%fused_computation.11 | convolution fusion | flops 872415232 | bytes 6094848 | tf_op jit(solution)/shard_map/dot_general | solution.py:49
  185.4 0.0 all-to-all-done.6
  185.4 3.4 %add_convert_fusion = bf16[1024,1024]{1,0:T(8,128)(2,1)S(1)} fusion(f32[1024,1024]{1,0:T(8,128)} %fusion.5, bf16[1024,416]{1,0:T(8,128)(2,1)S(1)} %bitcast.17, bf16[832,1024]{1,0:T(8,128)(2,1)S(1)} %copy-done), kind=kOutput, calls=%fused_computation.2 | convolution fusion | flops 874512384 | bytes 8192000 | tf_op jit(solution)/shard_map/dot_general | solution.py:50
  188.9 0.3 copy.15
  189.1 29.6 %all_to_all.53 = bf16[8,4,32,1024]{3,2,0,1:T(8,128)(2,1)S(1)} all-to-all(bf16[8,4,32,1024]{3,2,0,1:T(8,128)(2,1)S(1)} %copy.15), channel_id=1, replica_groups=mesh['z'=8,'x'=4,'y'=8,'core'=2] {'x'}, dimensions={1} | all-to-all | bytes 4194304 | tf_op jit(solution)/shard_map/all_to_all | solution.py:53
  218.7 0.4 reduce_sum.77
  219.2 19.7 %all_to_all.54 = bf16[8,32,1024]{2,1,0:T(8,128)(2,1)S(1)} all-to-all(bf16[8,32,1024]{2,1,0:T(8,128)(2,1)S(1)} %reduce_sum.77), channel_id=1, replica_groups=mesh['z'=8,'x'=4,'y'=8,'core'=2] {'z'}, dimensions={0} | all-to-all | bytes 1048576 | tf_op jit(solution)/shard_map/all_to_all | solution.py:56
  238.8 0.7 reduce_sum.78
  (3 shorter events, 0.0 us)
Async XLA Ops:
  62.7 0.7 copy-start.1
  63.4 1.5 copy-start.2
  63.4 2.0 copy-start.3
  76.3 14.7 %all-to-all-start.5 = ((f32[8,1,64]{2,1,0:T(1,128)}), f32[8,1,64]{2,1,0:T(1,128)S(1)}, u32[]{:S(2)}, u32[]{:S(2)}) async-start(f32[8,1,64]{2,1,0:T(1,128)} %bitcast.2), calls=%async_computation.5 | async-start | bytes 8192 | tf_op jit(solution)/shard_map/all_to_all | solution.py:39
  91.0 45.5 %all-to-all-start.3 = ((bf16[8,64,1664]{2,1,0:T(8,128)(2,1)}), bf16[8,64,1664]{2,1,0:T(8,128)(2,1)S(1)}, u32[]{:S(2)}, u32[]{:S(2)}) async-start(bf16[8,64,1664]{2,1,0:T(8,128)(2,1)} %reduce_sum.72), calls=%async_computation.3 | async-start | bytes 3407872 | tf_op jit(solution)/shard_map/all_to_all | solution.py:36
  137.0 45.3 %copy-start = (bf16[832,1024]{1,0:T(8,128)(2,1)S(1)}, bf16[832,1024]{1,0:T(8,128)(2,1)}, u32[]{:S(2)}) copy-start(bf16[832,1024]{1,0:T(8,128)(2,1)} %param.9) | copy-start | bytes 5111812
  138.1 47.4 %all-to-all-start.6 = ((bf16[16,64,416]{2,1,0:T(8,128)(2,1)}), bf16[16,64,416]{2,1,0:T(8,128)(2,1)S(1)}, u32[]{:S(2)}, u32[]{:S(2)}) async-start(bf16[16,64,416]{2,1,0:T(8,128)(2,1)} %stack.2), calls=%async_computation.6 | async-start | bytes 2097152 | tf_op jit(solution)/shard_map/all_to_all | solution.py:46
